TPU v7x, 32 devices: a whole 2x2x4 slice. The times are simulated.
32 devices in a mesh: grad: 4 (over y, x), col: 8 (over z, core).
Axes of the slice: x: 2, y: 2, z: 4, core: 2. Of those that a mesh axis runs over, the one named last changes fastest.
Arguments:
- gradient: bfloat16 [16384, 53248], P(('grad', 'col'))
- test_matrix: bfloat16 [16384, 256], P(('grad', 'col')), may hold values from -6 to 6
Outputs:
- low_rank: float32 [16384, 256], P(('grad', 'col'))
- projector: float32 [53248, 256], P('col')
All inputs are finite; a program needn't handle non-finite values.
Results may differ from a plain program's by a relative error of at most 0.008.
Values may be sent and summed in bfloat16 or wider, within the bound.
No kernel may reach another device: no remote copies, remote signals or barrier semaphores. Data moves between devices by JAX's collectives and lax.ppermute only.
A program may use at most 256 MiB of HBM per device.

v0:
```python
import math
import jax
import jax.numpy as jnp
from jax import lax
from jax.sharding import PartitionSpec as P

FF = 53248
POWER = 2


def orthonormal(matrix, reduce_gram):
    partial_gram = lax.dot_general(
        matrix,
        matrix,
        (((0,), (0,)), ((), ())),
        precision=lax.Precision.HIGHEST,
        preferred_element_type=jnp.float32,
    )
    gram = reduce_gram(partial_gram)
    lower_factor = jnp.linalg.cholesky(gram)
    return lax.linalg.triangular_solve(
        lower_factor, matrix, left_side=False, lower=True, transpose_a=True
    )


def gram_over_columns(partial_gram):
    return lax.psum(partial_gram, "col")


def shards(gradient, test_matrix):
    blocks = lax.all_to_all(gradient, "col", split_axis=1, concat_axis=0, tiled=True)

    def add_sketch(row_piece):
        return lax.dot_general(
            blocks, row_piece, (((0,), (0,)), ((), ())), preferred_element_type=jnp.float32
        )

    sketch = add_sketch(lax.all_gather(test_matrix, "col", axis=0, tiled=True))
    for iteration in range(POWER + 1):
        summed = lax.psum(sketch, "grad")
        basis_block = orthonormal(summed, gram_over_columns)
        basis_bf = basis_block.astype(jnp.bfloat16)
        reduced = lax.psum_scatter(
            jnp.dot(blocks, basis_bf, preferred_element_type=jnp.float32),
            "col",
            scatter_dimension=0,
            tiled=True,
        )
        if iteration < POWER:
            reduced_bf = reduced.astype(jnp.bfloat16)
            sketch = add_sketch(lax.all_gather(reduced_bf, "col", axis=0, tiled=True))
    return (reduced, basis_block * math.sqrt(FF))


def solution(mesh):
    return jax.shard_map(
        shards,
        mesh=mesh,
        in_specs=(P(("grad", "col"), None), P(("grad", "col"), None)),
        out_specs=(P(("grad", "col"), None), P("col", None)),
        check_vma=False,
    )
```

profile of v0, /device:TPU:0, one launch (start us, length us, event | category | flops | bytes accessed | tf_op | source)
XLA Modules:
  0.0 2602.8 jit_solution(11232503956803364355)
XLA Ops:
  7.2 70.6 %copy.20 = bf16[512,53248]{0,1:T(8,128)(2,1)} copy(bf16[512,53248]{1,0:T(8,128)(2,1)} %param.5) | data formatting | bytes 109051904 | tf_op args[0]
  87.4 1189.5 %all-to-all-done = bf16[512,8,6656]{0,2,1:T(8,128)(2,1)} async-done(((bf16[512,8,6656]{0,2,1:T(8,128)(2,1)}), bf16[512,8,6656]{0,2,1:T(8,128)(2,1)}, u32[]{:S(2)}, u32[]{:S(2)}) %all-to-all-start) | async-done | bytes 54525984 | tf_op jit(solution)/shard_map/all_to_all | solution.py:31
  1276.9 64.6 %copy.21 = bf16[8,512,6656]{2,1,0:T(8,128)(2,1)} copy(bf16[8,512,6656]{1,2,0:T(8,128)(2,1)} %bitcast.1) | data formatting | bytes 109051904 | tf_op jit(solution)/shard_map/all_to_all | solution.py:31
  1341.5 25.8 fusion.41
  1367.7 146.1 %all-reduce.8.cloned.1.call-done = f32[6656,256]{1,0:T(8,128)} async-done(((f32[6656,256]{1,0:T(8,128)}), f32[6656,256]{1,0:T(8,128)}) %all-reduce.8.cloned.1.call-update) | async-done | bytes 6815760 | tf_op jit(solution)/shard_map/psum | solution.py:40
  1531.0 55.0 %all-reduce.10.cloned.1.call-done = f32[256,256]{0,1:T(8,128)} async-done(((f32[256,256]{0,1:T(8,128)}), f32[256,256]{0,1:T(8,128)}) %all-reduce.10.cloned.1.call-update) | async-done | bytes 262160 | tf_op jit(solution)/shard_map/psum | solution.py:27
  1628.9 19.7 custom-call.16
  1664.7 24.3 convolution_bitcast_fusion.4
  1689.1 49.1 %reduce-scatter.4.cloned.1.call-done = f32[512,256]{0,1:T(8,128)} async-done(((f32[4096,256]{0,1:T(8,128)}), f32[512,256]{0,1:T(8,128)}) %reduce-scatter.4.cloned.1.call-update) | async-done | bytes 524304 | tf_op jit(solution)/shard_map/reduce_scatter | solution.py:43
  1740.1 27.8 %all-gather.6.cloned.1.call-done = bf16[4096,256]{0,1:T(8,128)(2,1)} async-done(((bf16[512,256]{0,1:T(8,128)(2,1)}), bf16[4096,256]{0,1:T(8,128)(2,1)}) %all-gather.6.cloned.1.call-update) | async-done | bytes 2097168 | tf_op jit(solution)/shard_map/all_gather | solution.py:51
  1767.9 25.5 convolution_bitcast_fusion.1
  1793.5 146.3 %all-reduce.12.cloned.1.call-done = f32[6656,256]{0,1:T(8,128)} async-done(((f32[6656,256]{0,1:T(8,128)}), f32[6656,256]{0,1:T(8,128)}) %all-reduce.12.cloned.1.call-update) | async-done | bytes 6815760 | tf_op jit(solution)/shard_map/psum | solution.py:40
  1939.8 19.3 fusion.43
  1959.6 55.1 %all-reduce.14.cloned.1.call-done = f32[256,256]{0,1:T(8,128)} async-done(((f32[256,256]{0,1:T(8,128)}), f32[256,256]{0,1:T(8,128)}) %all-reduce.14.cloned.1.call-update) | async-done | bytes 262160 | tf_op jit(solution)/shard_map/psum | solution.py:27
  2058.1 19.7 custom-call.18
  2091.4 24.5 convolution_bitcast_fusion.3
  2116.0 49.1 %reduce-scatter.6.cloned.1.call-done = f32[512,256]{0,1:T(8,128)} async-done(((f32[4096,256]{0,1:T(8,128)}), f32[512,256]{0,1:T(8,128)}) %reduce-scatter.6.cloned.1.call-update) | async-done | bytes 524304 | tf_op jit(solution)/shard_map/reduce_scatter | solution.py:43
  2167.0 28.0 %all-gather.8.cloned.1.call-done = bf16[4096,256]{0,1:T(8,128)(2,1)} async-done(((bf16[512,256]{0,1:T(8,128)(2,1)}), bf16[4096,256]{0,1:T(8,128)(2,1)}) %all-gather.8.cloned.1.call-update) | async-done | bytes 2097168 | tf_op jit(solution)/shard_map/all_gather | solution.py:51
  2194.9 25.5 convolution_bitcast_fusion
  2220.5 146.3 %all-reduce.16.cloned.1.call-done = f32[6656,256]{0,1:T(8,128)} async-done(((f32[6656,256]{0,1:T(8,128)}), f32[6656,256]{0,1:T(8,128)}) %all-reduce.16.cloned.1.call-update) | async-done | bytes 6815760 | tf_op jit(solution)/shard_map/psum | solution.py:40
  2386.6 55.1 %all-reduce.18.cloned.1.call-done = f32[256,256]{0,1:T(8,128)} async-done(((f32[256,256]{0,1:T(8,128)}), f32[256,256]{0,1:T(8,128)}) %all-reduce.18.cloned.1.call-update) | async-done | bytes 262160 | tf_op jit(solution)/shard_map/psum | solution.py:27
  2485.2 19.7 custom-call.20
  2519.2 25.4 convolution_bitcast_fusion.2
  2558.0 35.7 %reduce-scatter.8.cloned.1.call-done = f32[512,256]{0,1:T(8,128)} async-done(((f32[4096,256]{0,1:T(8,128)}), f32[512,256]{0,1:T(8,128)}) %reduce-scatter.8.cloned.1.call-update) | async-done | bytes 524304 | tf_op jit(solution)/shard_map/reduce_scatter | solution.py:43
  (121 shorter events, 248.2 us)
Async XLA Ops:
  77.8 1199.1 %all-to-all-start = ((bf16[512,8,6656]{0,2,1:T(8,128)(2,1)}), bf16[512,8,6656]{0,2,1:T(8,128)(2,1)}, u32[]{:S(2)}, u32[]{:S(2)}) async-start(bf16[512,8,6656]{0,2,1:T(8,128)(2,1)} %bitcast.124), calls=%async_computation | async-start | bytes 109051904 | tf_op jit(solution)/shard_map/all_to_all | solution.py:31
  86.6 1254.9 %all-gather.4.cloned.1.call-start = ((), (), s32[]{:S(2)}) async-start(), calls=%async_computation.4 | async-start | bytes 2359296 | tf_op jit(solution)/shard_map/all_gather | solution.py:38
  87.3 1426.5 %all-reduce.8.cloned.1.call-start = ((), (), s32[]{:S(2)}) async-start(), calls=%async_computation.5 | async-start | bytes 13631488 | tf_op jit(solution)/shard_map/psum | solution.py:40
  1367.4 218.6 %all-reduce.10.cloned.1.call-start = ((), (), s32[]{:S(2)}) async-start(), calls=%async_computation.6 | async-start | bytes 524288 | tf_op jit(solution)/shard_map/psum | solution.py:27
  1530.4 207.8 %reduce-scatter.4.cloned.1.call-start = ((), (), s32[]{:S(2)}) async-start(), calls=%async_computation.7 | async-start | bytes 4718592 | tf_op jit(solution)/shard_map/reduce_scatter | solution.py:43
  1628.2 0.7 copy-start.4
  1648.5 5.2 copy-start
  1689.1 78.8 %all-gather.6.cloned.1.call-start = ((), (), s32[]{:S(2)}) async-start(), calls=%async_computation.8 | async-start | bytes 2359296 | tf_op jit(solution)/shard_map/all_gather | solution.py:51
  1740.0 199.8 %all-reduce.12.cloned.1.call-start = ((), (), s32[]{:S(2)}) async-start(), calls=%async_computation.9 | async-start | bytes 13631488 | tf_op jit(solution)/shard_map/psum | solution.py:40
  1793.4 221.3 %all-reduce.14.cloned.1.call-start = ((), (), s32[]{:S(2)}) async-start(), calls=%async_computation.10 | async-start | bytes 524288 | tf_op jit(solution)/shard_map/psum | solution.py:27
  1959.1 206.0 %reduce-scatter.6.cloned.1.call-start = ((), (), s32[]{:S(2)}) async-start(), calls=%async_computation.11 | async-start | bytes 4718592 | tf_op jit(solution)/shard_map/reduce_scatter | solution.py:43
  2057.4 0.7 copy-start.5
  2077.8 5.2 copy-start.2
  2116.0 79.0 %all-gather.8.cloned.1.call-start = ((), (), s32[]{:S(2)}) async-start(), calls=%async_computation.12 | async-start | bytes 2359296 | tf_op jit(solution)/shard_map/all_gather | solution.py:51
  2166.9 199.9 %all-reduce.16.cloned.1.call-start = ((), (), s32[]{:S(2)}) async-start(), calls=%async_computation.13 | async-start | bytes 13631488 | tf_op jit(solution)/shard_map/psum | solution.py:40
  2220.5 221.3 %all-reduce.18.cloned.1.call-start = ((), (), s32[]{:S(2)}) async-start(), calls=%async_computation.14 | async-start | bytes 524288 | tf_op jit(solution)/shard_map/psum | solution.py:27
  2386.2 207.5 %reduce-scatter.8.cloned.1.call-start = ((), (), s32[]{:S(2)}) async-start(), calls=%async_computation.15 | async-start | bytes 4718592 | tf_op jit(solution)/shard_map/reduce_scatter | solution.py:43
  2484.5 0.7 copy-start.3
  2504.9 5.2 copy-start.1
Sparse Core Ops, SparseCore 0:
  89.0 49.5 all-gather.3
  1367.5 146.2 all-reduce.7
  1530.6 55.4 all-reduce.9
  1689.2 48.9 reduce-scatter.3
  1740.2 27.5 all-gather.5
  1793.5 146.1 all-reduce.11
  1959.2 55.4 all-reduce.13
  2116.1 48.9 reduce-scatter.5
  2167.3 27.6 all-gather.7
  2220.6 146.1 all-reduce.15
  2386.3 55.4 all-reduce.17
  2544.7 48.9 reduce-scatter.7
where the time goes:
time: 2610 us; the launch traced here: 2600 us
  waiting for transfers between devices  1980 us (76%)
  matrix products  252 us (10%)
  other arithmetic  174 us (7%)
  local copies, waits for them, and re-layouts  163 us (6%)
    all_to_all x1, waiting for transfers between devices, shards(): lax.all_to_all(gradient, 'col', split_axis=1, concat_axis=0, tiled=True)  1190 us
    psum x3, waiting for transfers between devices, shards(): summed = lax.psum(sketch, 'grad')  439 us
    psum x3, waiting for transfers between devices, gram_over_columns(): return lax.psum(partial_gram, 'col')  165 us
    reduce_scatter x3, waiting for transfers between devices, shards(): lax.psum_scatter(jnp.dot(blocks, basis_bf, preferred_element_type=jnp.flo...  134 us
    another operation x20, other arithmetic, orthonormal(): lower_factor = jnp.linalg.cholesky(gram)  103 us
    unnamed x15, local copies, waits for them, and re-layouts  82.9 us
    dot_general x3, matrix products, add_sketch(): lax.dot_general(blocks, row_piece, (((0,), (0,)), ((), ())), preferred_el...  76.9 us
    dot_general x3, matrix products, shards(): jnp.dot(blocks, basis_bf, preferred_element_type=jnp.float32)  74.2 us
  transfers between devices with their start and end apart: 13, of which 12 were waited for; matrix products, arithmetic and copies ran while one was open for 3% of the time, Pallas kernels for 0%

commit v1 on v0

--- a/solution.py
+++ b/solution.py
@@ -6,6 +6,12 @@
 
 FF = 53248
 POWER = 2
+
+
+def summed_here(x, axis):
+    parts = lax.all_gather(x, axis, axis=0, tiled=False)
+    total = parts.sum(axis=0)
+    return total
 
 
 def orthonormal(matrix, reduce_gram):
@@ -24,7 +30,7 @@
 
 
 def gram_over_columns(partial_gram):
-    return lax.psum(partial_gram, "col")
+    return summed_here(partial_gram, "col")
 
 
 def shards(gradient, test_matrix):

time: 2610 us -> 2530 us (0.969)
  waiting for transfers between devices: 1980 us -> 1910 us
    psum x3 -> x0, waiting for transfers between devices: 165 us -> none  [gram_over_columns(): return lax.psum(partial_gram, 'col')]
    all_gather x0 -> x3, waiting for transfers between devices: none -> 86.4 us  [summed_here(): parts = lax.all_gather(x, axis, axis=0, tiled=False)]
where the time goes in v1:
time: 2530 us; the launch traced here: 2520 us
  waiting for transfers between devices  1910 us (75%)
  matrix products  251 us (10%)
  other arithmetic  176 us (7%)
  local copies, waits for them, and re-layouts  160 us (6%)
    all_to_all x1, waiting for transfers between devices, shards(): lax.all_to_all(gradient, 'col', split_axis=1, concat_axis=0, tiled=True)  1190 us
    psum x3, waiting for transfers between devices, shards(): summed = lax.psum(sketch, 'grad')  439 us
    reduce_scatter x3, waiting for transfers between devices, shards(): lax.psum_scatter(jnp.dot(blocks, basis_bf, preferred_element_type=jnp.flo...  135 us
    another operation x20, other arithmetic, orthonormal(): lower_factor = jnp.linalg.cholesky(gram)  103 us
    all_gather x3, waiting for transfers between devices, summed_here(): parts = lax.all_gather(x, axis, axis=0, tiled=False)  86.4 us
    unnamed x15, local copies, waits for them, and re-layouts  82.9 us
    dot_general x3, matrix products, add_sketch(): lax.dot_general(blocks, row_piece, (((0,), (0,)), ((), ())), preferred_el...  76.9 us
    dot_general x3, matrix products, shards(): jnp.dot(blocks, basis_bf, preferred_element_type=jnp.float32)  74.2 us
  transfers between devices with their start and end apart: 13, of which 12 were waited for; matrix products, arithmetic and copies ran while one was open for 3% of the time, Pallas kernels for 0%

profile of v1, /device:TPU:0, one launch (start us, length us, event | category | flops | bytes accessed | tf_op | source)
XLA Modules:
  0.0 2524.1 jit_solution(8219104100991157887)
XLA Ops:
  7.2 70.6 %copy.23 = bf16[512,53248]{0,1:T(8,128)(2,1)} copy(bf16[512,53248]{1,0:T(8,128)(2,1)} %param.5) | data formatting | bytes 109051904 | tf_op args[0]
  87.4 1189.5 %all-to-all-done = bf16[512,8,6656]{0,2,1:T(8,128)(2,1)} async-done(((bf16[512,8,6656]{0,2,1:T(8,128)(2,1)}), bf16[512,8,6656]{0,2,1:T(8,128)(2,1)}, u32[]{:S(2)}, u32[]{:S(2)}) %all-to-all-start) | async-done | bytes 54525984 | tf_op jit(solution)/shard_map/all_to_all | solution.py:37
  1276.9 64.6 %copy.24 = bf16[8,512,6656]{2,1,0:T(8,128)(2,1)} copy(bf16[8,512,6656]{1,2,0:T(8,128)(2,1)} %bitcast.1) | data formatting | bytes 109051904 | tf_op jit(solution)/shard_map/all_to_all | solution.py:37
  1341.5 25.8 %fusion.41 = f32[6656,256]{1,0:T(8,128)} fusion(bf16[4096,6656]{1,0:T(8,128)(2,1)} %bitcast.128, bf16[4096,256]{1,0:T(8,128)(2,1)} %all-gather.10.cloned.1.call-done), kind=kOutput, calls=%fused_computation.93 | convolution fusion | flops 13958643712 | bytes 63438848 | tf_op jit(solution)/shard_map/dot_general | solution.py:40
  1367.7 146.1 %all-reduce.5.cloned.1.call-done = f32[6656,256]{1,0:T(8,128)} async-done(((f32[6656,256]{1,0:T(8,128)}), f32[6656,256]{1,0:T(8,128)}) %all-reduce.5.cloned.1.call-update) | async-done | bytes 6815760 | tf_op jit(solution)/shard_map/psum | solution.py:46
  1530.4 28.7 %all-gather.16.cloned.1.call-done = f32[2048,256]{1,0:T(8,128)} async-done(((f32[256,256]{1,0:T(8,128)}), f32[2048,256]{1,0:T(8,128)}) %all-gather.16.cloned.1.call-update) | async-done | bytes 2097168 | tf_op jit(solution)/shard_map/all_gather | solution.py:12
  1601.9 19.7 custom-call.16
  1637.8 24.3 convolution_bitcast_fusion.4
  1662.2 49.4 %reduce-scatter.4.cloned.1.call-done = f32[512,256]{0,1:T(8,128)} async-done(((f32[4096,256]{0,1:T(8,128)}), f32[512,256]{0,1:T(8,128)}) %reduce-scatter.4.cloned.1.call-update) | async-done | bytes 524304 | tf_op jit(solution)/shard_map/reduce_scatter | solution.py:49
  1713.4 27.8 %all-gather.12.cloned.1.call-done = bf16[4096,256]{0,1:T(8,128)(2,1)} async-done(((bf16[512,256]{0,1:T(8,128)(2,1)}), bf16[4096,256]{0,1:T(8,128)(2,1)}) %all-gather.12.cloned.1.call-update) | async-done | bytes 2097168 | tf_op jit(solution)/shard_map/all_gather | solution.py:57
  1741.3 25.5 %convolution_bitcast_fusion.1 = f32[6656,256]{0,1:T(8,128)} fusion(bf16[4096,256]{0,1:T(8,128)(2,1)} %all-gather.12.cloned.1.call-done, bf16[4096,6656]{1,0:T(8,128)(2,1)} %bitcast.130), kind=kOutput, calls=%fused_computation.7 | convolution fusion | flops 13958643712 | bytes 63438848 | tf_op jit(solution)/shard_map/dot_general | solution.py:40
  1766.9 146.3 %all-reduce.7.cloned.1.call-done = f32[6656,256]{0,1:T(8,128)} async-done(((f32[6656,256]{0,1:T(8,128)}), f32[6656,256]{0,1:T(8,128)}) %all-reduce.7.cloned.1.call-update) | async-done | bytes 6815760 | tf_op jit(solution)/shard_map/psum | solution.py:46
  1913.2 19.3 fusion.43
  1933.0 28.8 %all-gather.18.cloned.1.call-done = f32[2048,256]{1,0:T(8,128)} async-done(((f32[256,256]{1,0:T(8,128)}), f32[2048,256]{1,0:T(8,128)}) %all-gather.18.cloned.1.call-update) | async-done | bytes 2097168 | tf_op jit(solution)/shard_map/all_gather | solution.py:12
  2005.1 19.7 custom-call.18
  2038.4 24.5 convolution_bitcast_fusion.3
  2063.0 49.4 %reduce-scatter.6.cloned.1.call-done = f32[512,256]{0,1:T(8,128)} async-done(((f32[4096,256]{0,1:T(8,128)}), f32[512,256]{0,1:T(8,128)}) %reduce-scatter.6.cloned.1.call-update) | async-done | bytes 524304 | tf_op jit(solution)/shard_map/reduce_scatter | solution.py:49
  2114.3 28.0 %all-gather.14.cloned.1.call-done = bf16[4096,256]{0,1:T(8,128)(2,1)} async-done(((bf16[512,256]{0,1:T(8,128)(2,1)}), bf16[4096,256]{0,1:T(8,128)(2,1)}) %all-gather.14.cloned.1.call-update) | async-done | bytes 2097168 | tf_op jit(solution)/shard_map/all_gather | solution.py:57
  2142.3 25.5 %convolution_bitcast_fusion = f32[6656,256]{0,1:T(8,128)} fusion(bf16[4096,256]{0,1:T(8,128)(2,1)} %all-gather.14.cloned.1.call-done, bf16[4096,6656]{1,0:T(8,128)(2,1)} %bitcast.132), kind=kOutput, calls=%fused_computation.6 | convolution fusion | flops 13958643712 | bytes 63438848 | tf_op jit(solution)/shard_map/dot_general | solution.py:40
  2167.9 146.3 %all-reduce.9.cloned.1.call-done = f32[6656,256]{0,1:T(8,128)} async-done(((f32[6656,256]{0,1:T(8,128)}), f32[6656,256]{0,1:T(8,128)}) %all-reduce.9.cloned.1.call-update) | async-done | bytes 6815760 | tf_op jit(solution)/shard_map/psum | solution.py:46
  2334.0 28.8 %all-gather.20.cloned.1.call-done = f32[2048,256]{1,0:T(8,128)} async-done(((f32[256,256]{1,0:T(8,128)}), f32[2048,256]{1,0:T(8,128)}) %all-gather.20.cloned.1.call-update) | async-done | bytes 2097168 | tf_op jit(solution)/shard_map/all_gather | solution.py:12
  2406.1 19.7 custom-call.20
  2440.1 25.4 %convolution_bitcast_fusion.2 = f32[4096,256]{0,1:T(8,128)} fusion(bf16[4096,6656]{1,0:T(8,128)(2,1)} %bitcast.133, f32[6656,128]{0,1:T(8,128)} %fusion.12, f32[6656,128]{0,1:T(8,128)S(1)} %bitcast.134), kind=kOutput, calls=%fused_computation.16 | convolution fusion | flops 13965459456 | bytes 65536000 | tf_op jit(solution)/shard_map/dot_general | solution.py:50
  2479.0 36.0 %reduce-scatter.8.cloned.1.call-done = f32[512,256]{0,1:T(8,128)} async-done(((f32[4096,256]{0,1:T(8,128)}), f32[512,256]{0,1:T(8,128)}) %reduce-scatter.8.cloned.1.call-update) | async-done | bytes 524304 | tf_op jit(solution)/shard_map/reduce_scatter | solution.py:49
  (124 shorter events, 247.3 us)
Async XLA Ops:
  77.8 1199.1 %all-to-all-start = ((bf16[512,8,6656]{0,2,1:T(8,128)(2,1)}), bf16[512,8,6656]{0,2,1:T(8,128)(2,1)}, u32[]{:S(2)}, u32[]{:S(2)}) async-start(bf16[512,8,6656]{0,2,1:T(8,128)(2,1)} %bitcast.127), calls=%async_computation | async-start | bytes 109051904 | tf_op jit(solution)/shard_map/all_to_all | solution.py:37
  86.6 1254.9 %all-gather.10.cloned.1.call-start = ((), (), s32[]{:S(2)}) async-start(), calls=%async_computation.4 | async-start | bytes 2359296 | tf_op jit(solution)/shard_map/all_gather | solution.py:44
  87.3 1426.5 %all-reduce.5.cloned.1.call-start = ((), (), s32[]{:S(2)}) async-start(), calls=%async_computation.5 | async-start | bytes 13631488 | tf_op jit(solution)/shard_map/psum | solution.py:46
  1367.4 191.8 %all-gather.16.cloned.1.call-start = ((), (), s32[]{:S(2)}) async-start(), calls=%async_computation.13 | async-start | bytes 2359296 | tf_op jit(solution)/shard_map/all_gather | solution.py:12
  1529.9 181.7 %reduce-scatter.4.cloned.1.call-start = ((), (), s32[]{:S(2)}) async-start(), calls=%async_computation.6 | async-start | bytes 4718592 | tf_op jit(solution)/shard_map/reduce_scatter | solution.py:49
  1601.2 0.7 copy-start.4
  1621.5 5.2 copy-start
  1662.1 79.2 %all-gather.12.cloned.1.call-start = ((), (), s32[]{:S(2)}) async-start(), calls=%async_computation.7 | async-start | bytes 2359296 | tf_op jit(solution)/shard_map/all_gather | solution.py:57
  1713.4 199.8 %all-reduce.7.cloned.1.call-start = ((), (), s32[]{:S(2)}) async-start(), calls=%async_computation.8 | async-start | bytes 13631488 | tf_op jit(solution)/shard_map/psum | solution.py:46
  1766.8 195.0 %all-gather.18.cloned.1.call-start = ((), (), s32[]{:S(2)}) async-start(), calls=%async_computation.14 | async-start | bytes 2359296 | tf_op jit(solution)/shard_map/all_gather | solution.py:12
  1932.5 179.9 %reduce-scatter.6.cloned.1.call-start = ((), (), s32[]{:S(2)}) async-start(), calls=%async_computation.9 | async-start | bytes 4718592 | tf_op jit(solution)/shard_map/reduce_scatter | solution.py:49
  2004.4 0.7 copy-start.5
  2024.8 5.2 copy-start.2
  2062.9 79.3 %all-gather.14.cloned.1.call-start = ((), (), s32[]{:S(2)}) async-start(), calls=%async_computation.10 | async-start | bytes 2359296 | tf_op jit(solution)/shard_map/all_gather | solution.py:57
  2114.2 199.9 %all-reduce.9.cloned.1.call-start = ((), (), s32[]{:S(2)}) async-start(), calls=%async_computation.11 | async-start | bytes 13631488 | tf_op jit(solution)/shard_map/psum | solution.py:46
  2167.8 195.0 %all-gather.20.cloned.1.call-start = ((), (), s32[]{:S(2)}) async-start(), calls=%async_computation.15 | async-start | bytes 2359296 | tf_op jit(solution)/shard_map/all_gather | solution.py:12
  2333.5 181.4 %reduce-scatter.8.cloned.1.call-start = ((), (), s32[]{:S(2)}) async-start(), calls=%async_computation.12 | async-start | bytes 4718592 | tf_op jit(solution)/shard_map/reduce_scatter | solution.py:49
  2405.4 0.7 copy-start.3
  2425.8 5.2 copy-start.1
Sparse Core Ops, SparseCore 0:
  89.0 49.5 all-gather.9
  1367.5 146.2 all-reduce.4
  1530.0 29.1 all-gather.15
  1662.2 49.3 reduce-scatter.3
  1713.6 27.6 all-gather.11
  1767.0 146.1 all-reduce.6
  1932.6 29.1 all-gather.17
  2063.1 49.3 reduce-scatter.5
  2114.6 27.6 all-gather.13
  2167.9 146.1 all-reduce.8
  2333.6 29.1 all-gather.19
  2465.6 49.3 reduce-scatter.7
